TPU v7x, 512 devices: a whole 4x4x16 slice. The times are simulated.
512 devices in a mesh: fsdp: 128 (over z, y, core), seq: 4 (over x).
Axes of the slice: x: 4, y: 4, z: 16, core: 2. Of those that a mesh axis runs over, the one named last changes fastest.
Arguments:
- tokens: bfloat16 [128, 512, 8192], P('fsdp', 'seq'), may hold values from -6 to 6
- queries: bfloat16 [128, 512, 8192], P('fsdp', None, 'seq'), may hold values from -6 to 6
- key_weight: bfloat16 [8192, 1024], P('fsdp', 'seq'), may hold values from -1 to 1
- u_factor: float32 [8192, 64], P('fsdp'), may hold values from -6 to 6
- v_factor: float32 [1024, 64], replicated, may hold values from -6 to 6
Outputs:
- update: float32 [8192, 1024], P('fsdp')
- losses: float32 [2], replicated
All inputs are finite; a program needn't handle non-finite values.
Results may differ from a plain program's by a relative error of at most 0.0003.
Values may be sent and summed in bfloat16 or wider, within the bound.
No kernel may reach another device: no remote copies, remote signals or barrier semaphores. Data moves between devices by JAX's collectives and lax.ppermute only.
A program may use at most 64 MiB of HBM per device.

v0:
```python
import math
import jax
import jax.numpy as jnp
from jax import lax
from jax.sharding import PartitionSpec as P

D = 8192
HQ = 64
HD = 128
R = 64
KD = 1024
GROUP = 8


def highest(left, right):
    return jnp.dot(left, right, precision=lax.Precision.HIGHEST, preferred_element_type=jnp.float32)


def solve_rows(rows, gram):
    lower = jnp.linalg.cholesky(gram)
    return lax.linalg.triangular_solve(lower, rows, left_side=False, lower=True, transpose_a=True)


def orthonormal(factor):
    for turn in range(2):
        factor = solve_rows(factor, highest(factor.T, factor))
    return factor


def orthonormal_map(factor):
    gram = highest(factor.T, factor)
    eye = jnp.eye(gram.shape[0], dtype=gram.dtype)
    first = lax.linalg.triangular_solve(
        jnp.linalg.cholesky(gram), eye, left_side=False, lower=True, transpose_a=True
    )
    second_gram = highest(first.T, highest(gram, first))
    second = lax.linalg.triangular_solve(
        jnp.linalg.cholesky(second_gram), eye, left_side=False, lower=True, transpose_a=True
    )
    return highest(factor, highest(first, second))


def split3(values):
    hi = lax.reduce_precision(values, exponent_bits=8, mantissa_bits=7)
    rest = values - hi
    mid = lax.reduce_precision(rest, exponent_bits=8, mantissa_bits=7)
    lo = rest - mid
    return [piece.astype(jnp.bfloat16) for piece in (hi, mid, lo)]


def total_over(values, axis):
    n = lax.axis_size(axis)
    spread = jnp.broadcast_to(values[None], (n,) + values.shape)
    return jnp.sum(lax.all_to_all(spread, axis, 0, 0, tiled=True), axis=0)


def local(tokens, queries, key_weight, u_factor, v_factor):
    n_seq = lax.axis_size("seq")
    me_seq = lax.axis_index("seq")
    me_fsdp = lax.axis_index("fsdp")
    slice_width = key_weight.shape[1]
    rows = u_factor.shape[0]
    packed = jnp.concatenate([key_weight] + split3(u_factor), axis=1)
    whole = lax.all_gather(packed, "fsdp", axis=0, tiled=True)
    x_local = tokens[0]
    chunk = x_local.shape[0]
    chunks = [x_local]
    for shift in range(1, n_seq):
        chunks.append(
            lax.ppermute(x_local, "seq", [(i, (i + shift) % n_seq) for i in range(n_seq)])
        )
    q_v = orthonormal(v_factor)
    weight_piece = whole[:, :slice_width]
    r = u_factor.shape[1]
    u_whole = (
        whole[:, slice_width : slice_width + r].astype(jnp.float32)
        + whole[:, slice_width + r : slice_width + 2 * r].astype(jnp.float32)
        + whole[:, slice_width + 2 * r :].astype(jnp.float32)
    )
    q_u = orthonormal_map(lax.optimization_barrier(u_whole))
    q_low = q_u.astype(jnp.bfloat16)
    both = jnp.concatenate([weight_piece, q_low], axis=1)
    col_start = me_seq * slice_width
    v_slice = lax.dynamic_slice_in_dim(q_v, col_start, slice_width, 0)
    prod = jnp.dot(jnp.concatenate(chunks, axis=0), both, preferred_element_type=jnp.float32)
    base = prod[:, :slice_width]
    side = prod[:, slice_width:]
    offset = 2.0 * highest(side, v_slice.T)
    keys = jnp.stack([base + offset, base - offset]).astype(jnp.bfloat16)
    length = keys.shape[1]
    block = (me_seq - jnp.arange(n_seq)) % n_seq
    key_pos = (block[:, None] * chunk + jnp.arange(chunk)[None, :]).reshape(length)
    local_kv = slice_width // HD
    query_rows = queries[0]
    query_heads = query_rows.reshape(length, local_kv, GROUP, HD).transpose(1, 2, 0, 3)
    key_heads = keys.reshape(2, length, local_kv, HD).transpose(2, 0, 1, 3)
    places = jnp.arange(length)
    causal = places[:, None] >= key_pos[None, :]
    factor_scale = 1.0 / math.sqrt(HD)

    def one_query_head(query_one, key_one):
        scores = (
            jnp.einsum("td,npd->ntp", query_one, key_one, preferred_element_type=jnp.float32)
            * factor_scale
        )
        scores = jnp.where(causal[None], scores, -1e30)
        top = jnp.max(scores, axis=-1)
        total = jnp.sum(jnp.where(causal[None], jnp.exp(scores - top[..., None]), 0.0), axis=-1)
        return jnp.sum(top + jnp.log(total), axis=1)

    def one_key_head(pair):
        group_queries, key_one = pair
        return jnp.sum(
            lax.map(lambda query_one: one_query_head(query_one, key_one), group_queries), axis=0
        )

    partial_sums = jnp.sum(lax.map(one_key_head, (query_heads, key_heads)), axis=0)
    sums = total_over(total_over(partial_sums, "fsdp"), "seq")
    losses = sums / (lax.axis_size("fsdp") * length * HQ)
    unit = math.sqrt(D * KD / R)
    u_rows = lax.dynamic_slice_in_dim(q_u, me_fsdp * rows, rows, 0)
    update = unit * highest(u_rows, q_v.T)
    return (update, losses)


def solution(mesh):
    in_specs = (
        P("fsdp", "seq", None),
        P("fsdp", None, "seq"),
        P("fsdp", "seq"),
        P("fsdp", None),
        P(),
    )
    out_specs = (P("fsdp", None), P())
    return jax.shard_map(local, mesh=mesh, in_specs=in_specs, out_specs=out_specs, check_vma=False)
```

profile of v0, /device:TPU:1, one launch (start us, length us, event | category | flops | bytes accessed | tf_op | source)
XLA Modules:
  0.0 288.8 jit_solution(2902003976088465910)
XLA Ops:
  9.7 3.9 %collective-permute-start = (bf16[128,8192]{1,0:T(8,128)(2,1)}, bf16[128,8192]{1,0:T(8,128)(2,1)}, u32[]{:S(2)}, u32[]{:S(2)}) collective-permute-start(bf16[128,8192]{1,0:T(8,128)(2,1)} %bitcast.114), channel_id=1, source_target_pairs={{0,1},{1,2},{2,3},{3,0},{4,5},{5,6},{6,7},{7,4},{8,9},{9,10},{10,1... | collective-permute-start | bytes 6291464 | tf_op jit(solution)/shard_map/ppermute | solution.py:70
  13.6 4.4 %collective-permute-start.1 = (bf16[128,8192]{1,0:T(8,128)(2,1)}, bf16[128,8192]{1,0:T(8,128)(2,1)}, u32[]{:S(2)}, u32[]{:S(2)}) collective-permute-start(bf16[128,8192]{1,0:T(8,128)(2,1)} %bitcast.115), channel_id=1, source_target_pairs={{0,2},{1,3},{2,0},{3,1},{4,6},{5,7},{6,4},{7,5},{8,10},{9,11},{10,... | collective-permute-start | bytes 6291464 | tf_op jit(solution)/shard_map/ppermute | solution.py:70
  18.0 3.1 %collective-permute-start.2 = (bf16[128,8192]{1,0:T(8,128)(2,1)}, bf16[128,8192]{1,0:T(8,128)(2,1)}, u32[]{:S(2)}, u32[]{:S(2)}) collective-permute-start(bf16[128,8192]{1,0:T(8,128)(2,1)} %bitcast.116), channel_id=1, source_target_pairs={{0,3},{1,0},{2,1},{3,2},{4,7},{5,4},{6,5},{7,6},{8,11},{9,8},{10,9... | collective-permute-start | bytes 6291464 | tf_op jit(solution)/shard_map/ppermute | solution.py:70
  21.5 5.8 %cholesky.96 = f32[64,64]{1,0:T(8,128)S(1)} custom-call(f32[64,64]{1,0:T(8,128)S(1)} %fusion.32), custom_call_target="Cholesky" | custom-call | tf_op jit(solution)/shard_map/jit(cholesky)/cholesky | solution.py:20
  28.7 4.9 %custom-call.12 = f32[1,64,64]{1,2,0:T(8,128)S(1)} custom-call(f32[1,64,64]{2,1,0:T(8,128)S(1)} %fusion.26), custom_call_target="InvertDiagBlocksLowerTriangular" | custom-call | tf_op jit(solution)/shard_map/triangular_solve/custom-call.2 | solution.py:21
  34.5 5.9 %cholesky.107 = f32[64,64]{1,0:T(8,128)S(1)} custom-call(f32[64,64]{1,0:T(8,128)S(1)} %fusion.30), custom_call_target="Cholesky" | custom-call | tf_op jit(solution)/shard_map/jit(cholesky)/cholesky | solution.py:20
  41.7 4.9 %custom-call.13 = f32[1,64,64]{1,2,0:T(8,128)S(1)} custom-call(f32[1,64,64]{2,1,0:T(8,128)S(1)} %fusion.27), custom_call_target="InvertDiagBlocksLowerTriangular" | custom-call | tf_op jit(solution)/shard_map/triangular_solve/custom-call.2 | solution.py:21
  46.6 2.5 copy.36
  50.3 114.1 %all-gather.2.cloned.1.call-done = bf16[8192,448]{1,0:T(8,128)(2,1)} async-done(((bf16[64,448]{1,0:T(8,128)(2,1)}), bf16[8192,448]{1,0:T(8,128)(2,1)}) %all-gather.2.cloned.1.call-update) | async-done | bytes 7340048 | tf_op jit(solution)/shard_map/all_gather | solution.py:64
  164.4 3.8 %convert_add_fusion = f32[8192,64]{1,0:T(8,128)S(1)} fusion(bf16[8192,448]{1,0:T(8,128)(2,1)} %all-gather.2.cloned.1.call-done), kind=kLoop, calls=%fused_computation.26 | loop fusion | flops 2621440 | bytes 5242880 | tf_op jit(solution)/shard_map/add | solution.py:76
  170.2 7.1 %fusion.44 = f32[64,64]{1,0:T(8,128)S(1)} fusion(f32[8192,64]{1,0:T(8,128)S(1)} %convert_add_fusion), kind=kOutput, calls=%fused_computation.88 | convolution fusion | flops 402653184 | bytes 2113536 | tf_op jit(solution)/shard_map/dot_general | solution.py:16
  177.4 5.8 %cholesky.74 = f32[64,64]{1,0:T(8,128)S(1)} custom-call(f32[64,64]{1,0:T(8,128)S(1)} %fusion.36), custom_call_target="Cholesky" | custom-call | tf_op jit(solution)/shard_map/jit(cholesky)/cholesky | solution.py:34
  184.6 4.9 %custom-call.10 = f32[1,64,64]{1,2,0:T(8,128)S(1)} custom-call(f32[1,64,64]{2,1,0:T(8,128)S(1)} %fusion.24), custom_call_target="InvertDiagBlocksLowerTriangular" | custom-call | tf_op jit(solution)/shard_map/triangular_solve/custom-call.0 | solution.py:33
  190.2 5.8 %cholesky.85 = f32[64,64]{1,0:T(8,128)S(1)} custom-call(f32[64,64]{1,0:T(8,128)S(1)} %fusion.34), custom_call_target="Cholesky" | custom-call | tf_op jit(solution)/shard_map/jit(cholesky)/cholesky | solution.py:38
  197.4 4.9 %custom-call.11 = f32[1,64,64]{1,2,0:T(8,128)S(1)} custom-call(f32[1,64,64]{2,1,0:T(8,128)S(1)} %fusion.25), custom_call_target="InvertDiagBlocksLowerTriangular" | custom-call | tf_op jit(solution)/shard_map/triangular_solve/custom-call.0 | solution.py:37
  202.8 8.5 %fusion.43 = (bf16[8192,64]{0,1:T(8,128)(2,1)S(1)}, f32[8192,64]{0,1:T(8,128)}) fusion(f32[8192,64]{1,0:T(8,128)} %copy-done.1, f32[64,64]{1,0:T(8,128)S(1)} %fusion.47), kind=kOutput, calls=%fused_computation.87 | convolution fusion | flops 403177472 | bytes 5259264 | tf_op jit(solution)/shard_map/dot_general | solution.py:16
  212.4 2.1 slice-done
  215.3 5.6 %fusion.9 = f32[512,320]{0,1:T(8,128)S(1)} fusion(bf16[128,8192]{1,0:T(8,128)(2,1)} %collective-permute-done.2, bf16[128,8192]{1,0:T(8,128)(2,1)} %collective-permute-done.1, bf16[128,8192]{1,0:T(8,128)(2,1)} %collective-permute-done, bf16[128,8192]{1,0:T(8,128)(2,1)S(1)} %bitcast.117, bf16[8192,64]{1,0:T(8,128)(2,1)S(1)} %copy.37, ...), kind=kOutput, calls=%fused_computation.15 | convolution fusion | flops 2728394752 | bytes 14286848 | tf_op jit(solution)/shard_map/dot_general | solution.py:85
  222.8 25.5 %while.23 = (s32[]{:T(128)}, f32[2,2]{1,0:T(2,128)S(1)}, bf16[2,8,512,128]{2,3,1,0:T(8,128)(2,1)}, bf16[2,2,512,128]{3,2,1,0:T(8,128)(2,1)S(1)}, s32[512]{0:T(51...) while((s32[]{:T(128)}, f32[2,2]{1,0:T(2,128)S(1)}, ...), condition=%wide.region_9.13_spmd.clone, body=%wide.region_2.12_spmd.clone.sunk | while | flops 138674192 | bytes 10115450 | solution.py:117
  225.1 10.4 %while.24 = (s32[]{:T(128)}, f32[8,2]{1,0:T(8,128)S(1)}, pred[512,512]{0,1:T(8,128)(4,1)S(1)}, bf16[8,512,128]{2,1,0:T(8,128)(2,1)S(1)}, bf16[2,512,128]{2,1,0:T(8,128)(2,1)S(1)}, /*index=5*/s32[]{:T(128)}, s32[]{:T(128)}) while((s32[]{:T(128)}, f32[8,2]{1,0:T(8,128)S(1)}, pred[512,512]{0,1:T(8,128)(4,1)S(1)}, ...), condition=%wide.region_7.10_spmd, body=%wide.region_3.0_spmd.sunk | while | flops 138412032 | bytes 5132397 | solution.py:114
  237.8 10.4 %while.24 = (s32[]{:T(128)}, f32[8,2]{1,0:T(8,128)S(1)}, pred[512,512]{0,1:T(8,128)(4,1)S(1)}, bf16[8,512,128]{2,1,0:T(8,128)(2,1)S(1)}, bf16[2,512,128]{2,1,0:T(8,128)(2,1)S(1)}, /*index=5*/s32[]{:T(128)}, s32[]{:T(128)}) while((s32[]{:T(128)}, f32[8,2]{1,0:T(8,128)S(1)}, pred[512,512]{0,1:T(8,128)(4,1)S(1)}, ...), condition=%wide.region_7.10_spmd, body=%wide.region_3.0_spmd.sunk | while | flops 138412032 | bytes 5132397 | solution.py:114
  248.9 9.6 %all-to-all-start = ((f32[128,1,2]{2,1,0:T(1,128)}), f32[128,1,2]{2,1,0:T(1,128)S(1)}, u32[]{:S(2)}, u32[]{:S(2)}) async-start(f32[128,1,2]{2,1,0:T(1,128)} %broadcast_in_dim.47), calls=%async_computation | async-start | bytes 131072 | tf_op jit(solution)/shard_map/all_to_all | solution.py:54
  260.5 12.9 %all-to-all-done = f32[128,1,2]{2,1,0:T(1,128)S(1)} async-done(((f32[128,1,2]{2,1,0:T(1,128)}), f32[128,1,2]{2,1,0:T(1,128)S(1)}, u32[]{:S(2)}, u32[]{:S(2)}) %all-to-all-start) | async-done | bytes 1056 | tf_op jit(solution)/shard_map/all_to_all | solution.py:54
  273.6 7.9 %all_to_all.12 = f32[4,1,2]{2,1,0:T(1,128)S(1)} all-to-all(f32[4,1,2]{2,1,0:T(1,128)S(1)} %broadcast_in_dim.48), channel_id=1, replica_groups=mesh['fsdp'=128,'seq'=4] {'seq'}, dimensions={0} | all-to-all | bytes 64 | tf_op jit(solution)/shard_map/all_to_all | solution.py:54
  (140 shorter events, 45.5 us)
Async XLA Ops:
  7.2 13.9 %copy-start = (f32[1024,64]{0,1:T(8,128)S(1)}, f32[1024,64]{0,1:T(8,128)}, u32[]{:S(2)}) copy-start(f32[1024,64]{0,1:T(8,128)} %param.18) | copy-start | bytes 786436
  7.2 39.4 %copy-start.2 = (bf16[1,512,2048]{2,1,0:T(8,128)(2,1)S(1)}, bf16[1,512,2048]{2,1,0:T(8,128)(2,1)}, u32[]{:S(2)}) copy-start(bf16[1,512,2048]{2,1,0:T(8,128)(2,1)} %param.15) | copy-start | bytes 6291460
  7.2 157.3 %all-gather.2.cloned.1.call-start = ((), (), s32[]{:S(2)}) async-start(), calls=%async_computation.2 | async-start | bytes 8454144 | tf_op jit(solution)/shard_map/all_gather | solution.py:64
  9.7 202.8 %collective-permute-start = (bf16[128,8192]{1,0:T(8,128)(2,1)}, bf16[128,8192]{1,0:T(8,128)(2,1)}, u32[]{:S(2)}, u32[]{:S(2)}) collective-permute-start(bf16[128,8192]{1,0:T(8,128)(2,1)} %bitcast.114), channel_id=1, source_target_pairs={{0,1},{1,2},{2,3},{3,0},{4,5},{5,6},{6,7},{7,4},{8,9},{9,10},{10,1... | collective-permute-start | bytes 6291464 | tf_op jit(solution)/shard_map/ppermute | solution.py:70
  13.6 198.8 %collective-permute-start.1 = (bf16[128,8192]{1,0:T(8,128)(2,1)}, bf16[128,8192]{1,0:T(8,128)(2,1)}, u32[]{:S(2)}, u32[]{:S(2)}) collective-permute-start(bf16[128,8192]{1,0:T(8,128)(2,1)} %bitcast.115), channel_id=1, source_target_pairs={{0,2},{1,3},{2,0},{3,1},{4,6},{5,7},{6,4},{7,5},{8,10},{9,11},{10,... | collective-permute-start | bytes 6291464 | tf_op jit(solution)/shard_map/ppermute | solution.py:70
  18.0 194.5 %collective-permute-start.2 = (bf16[128,8192]{1,0:T(8,128)(2,1)}, bf16[128,8192]{1,0:T(8,128)(2,1)}, u32[]{:S(2)}, u32[]{:S(2)}) collective-permute-start(bf16[128,8192]{1,0:T(8,128)(2,1)} %bitcast.116), channel_id=1, source_target_pairs={{0,3},{1,0},{2,1},{3,2},{4,7},{5,4},{6,5},{7,6},{8,11},{9,8},{10,9... | collective-permute-start | bytes 6291464 | tf_op jit(solution)/shard_map/ppermute | solution.py:70
  168.2 2.0 copy-start.1
  212.4 2.2 slice-start
  212.4 2.9 copy-start.4
  222.7 35.8 %copy-start.3 = (f32[1024,64]{0,1:T(8,128)S(1)}, f32[1024,64]{0,1:T(8,128)}, u32[]{:S(2)}) copy-start(f32[1024,64]{0,1:T(8,128)} %convolution_bitcast_fusion) | copy-start | bytes 786436
  248.9 24.5 %all-to-all-start = ((f32[128,1,2]{2,1,0:T(1,128)}), f32[128,1,2]{2,1,0:T(1,128)S(1)}, u32[]{:S(2)}, u32[]{:S(2)}) async-start(f32[128,1,2]{2,1,0:T(1,128)} %broadcast_in_dim.47), calls=%async_computation | async-start | bytes 131072 | tf_op jit(solution)/shard_map/all_to_all | solution.py:54
Sparse Core Ops, SparseCore 0:
  11.1 153.2 all-gather.1
where the time goes:
time: 289 us
  waiting for transfers between devices  127 us (44%)
  other arithmetic  67 us (23%)
  matrix products  36.8 us (13%)
  starting transfers between devices  21 us (7%)
  local copies, waits for them, and re-layouts  14.4 us (5%)
  between operations  14.4 us (5%)
  blocking collectives  7.89 us (3%)
    all_gather x1, waiting for transfers between devices, local(): whole = lax.all_gather(packed, 'fsdp', axis=0, tiled=True)  114 us
    dot_general x9, matrix products, highest(): jnp.dot(left, right, precision=lax.Precision.HIGHEST, preferred_element_t...  20.4 us
    another operation x6, other arithmetic, solve_rows(): lower = jnp.linalg.cholesky(gram)  13 us
    all_to_all x1, waiting for transfers between devices, total_over(): return jnp.sum(lax.all_to_all(spread, axis, 0, 0, tiled=True), axis=0)  12.9 us
    ppermute x3, starting transfers between devices, local(): lax.ppermute(x_local, 'seq', [(i, (i + shift) % n_seq) for i in range(n_s...  11.4 us
    another operation x4, other arithmetic, solve_rows(): lax.linalg.triangular_solve(lower, rows, left_side=False, lower=True, tra...  11.1 us
    all_to_all x1, starting transfers between devices, total_over(): return jnp.sum(lax.all_to_all(spread, axis, 0, 0, tiled=True), axis=0)  9.62 us
    reduce_sum x16, other arithmetic, one_query_head(): jnp.sum(jnp.where(causal[None], jnp.exp(scores - top[..., None]), 0.0), a...  9.15 us
  transfers between devices with their start and end apart: 5, of which 2 were waited for; matrix products, arithmetic and copies ran while one was open for 27% of the time, Pallas kernels for 0%

commit v1 on v0

--- a/solution.py
+++ b/solution.py
@@ -61,7 +61,9 @@
     slice_width = key_weight.shape[1]
     rows = u_factor.shape[0]
     packed = jnp.concatenate([key_weight] + split3(u_factor), axis=1)
-    whole = lax.all_gather(packed, "fsdp", axis=0, tiled=True)
+    whole = jnp.concatenate(
+        lax.all_to_all(jnp.stack([packed] * lax.axis_size("fsdp")), "fsdp", 0, 0), axis=0
+    )
     x_local = tokens[0]
     chunk = x_local.shape[0]
     chunks = [x_local]

time: 289 us -> 515 us (1.78)
  waiting for transfers between devices: 127 us -> 337 us
  starting transfers between devices: 21 us -> 43.9 us
  between operations: 14.4 us -> 0.99 us
  local copies, waits for them, and re-layouts: 14.4 us -> 20.2 us
    all_to_all x0 -> x1, waiting for transfers between devices: none -> 324 us  [local(): lax.all_to_all(jnp.stack([packed] * lax.axis_size('fsdp')), 'fsdp', 0, 0)]
    all_gather x1 -> x0, waiting for transfers between devices: 114 us -> none  [local(): whole = lax.all_gather(packed, 'fsdp', axis=0, tiled=True)]
    all_to_all x0 -> x1, starting transfers between devices: none -> 21 us  [local(): lax.all_to_all(jnp.stack([packed] * lax.axis_size('fsdp')), 'fsdp', 0, 0)]
  transfers between devices with their start and end apart: 5 -> 5, of which waited for: 2 -> 2; matrix products, arithmetic and copies ran while one was open for 27% -> 16% of each run, Pallas kernels for 0% -> 0%
where the time goes in v1:
time: 515 us; the launch traced here: 514 us
  waiting for transfers between devices  337 us (65%)
  other arithmetic  66.2 us (13%)
  starting transfers between devices  43.9 us (9%)
  matrix products  37.5 us (7%)
  local copies, waits for them, and re-layouts  20.2 us (4%)
  blocking collectives  7.94 us (2%)
    all_to_all x1, waiting for transfers between devices, local(): lax.all_to_all(jnp.stack([packed] * lax.axis_size('fsdp')), 'fsdp', 0, 0)  324 us
    all_to_all x1, starting transfers between devices, local(): lax.all_to_all(jnp.stack([packed] * lax.axis_size('fsdp')), 'fsdp', 0, 0)  21 us
    dot_general x9, matrix products, highest(): jnp.dot(left, right, precision=lax.Precision.HIGHEST, preferred_element_t...  20.3 us
    another operation x6, other arithmetic, solve_rows(): lower = jnp.linalg.cholesky(gram)  13 us
    all_to_all x1, waiting for transfers between devices, total_over(): return jnp.sum(lax.all_to_all(spread, axis, 0, 0, tiled=True), axis=0)  12.9 us
    all_to_all x1, starting transfers between devices, total_over(): return jnp.sum(lax.all_to_all(spread, axis, 0, 0, tiled=True), axis=0)  12.2 us
    another operation x4, other arithmetic, solve_rows(): lax.linalg.triangular_solve(lower, rows, left_side=False, lower=True, tra...  11.1 us
    ppermute x3, starting transfers between devices, local(): lax.ppermute(x_local, 'seq', [(i, (i + shift) % n_seq) for i in range(n_s...  10.7 us
  transfers between devices with their start and end apart: 5, of which 2 were waited for; matrix products, arithmetic and copies ran while one was open for 16% of the time, Pallas kernels for 0%

profile of v1, /device:TPU:1, one launch (start us, length us, event | category | flops | bytes accessed | tf_op | source)
XLA Modules:
  0.0 514.2 jit_solution(14461433863919634058)
XLA Ops:
  2.3 4.3 stack.8
  6.6 21.0 %all-to-all-start = ((bf16[128,64,448]{2,1,0:T(8,128)(2,1)}), bf16[128,64,448]{2,1,0:T(8,128)(2,1)}, u32[]{:S(2)}, u32[]{:S(2)}) async-start(bf16[128,64,448]{2,1,0:T(8,128)(2,1)} %stack.8), calls=%async_computation | async-start | bytes 16777216 | tf_op jit(solution)/shard_map/all_to_all | solution.py:65
  27.6 3.3 collective-permute-start
  30.9 4.4 collective-permute-start.1
  38.8 5.8 %cholesky.96 = f32[64,64]{1,0:T(8,128)S(1)} custom-call(f32[64,64]{1,0:T(8,128)S(1)} %fusion.32), custom_call_target="Cholesky" | custom-call | tf_op jit(solution)/shard_map/jit(cholesky)/cholesky | solution.py:20
  46.0 4.9 custom-call.12
  51.8 5.8 %cholesky.107 = f32[64,64]{1,0:T(8,128)S(1)} custom-call(f32[64,64]{1,0:T(8,128)S(1)} %fusion.30), custom_call_target="Cholesky" | custom-call | tf_op jit(solution)/shard_map/jit(cholesky)/cholesky | solution.py:20
  58.9 4.9 custom-call.13
  67.6 324.2 %all-to-all-done = bf16[128,64,448]{2,1,0:T(8,128)(2,1)} async-done(((bf16[128,64,448]{2,1,0:T(8,128)(2,1)}), bf16[128,64,448]{2,1,0:T(8,128)(2,1)}, u32[]{:S(2)}, u32[]{:S(2)}) %all-to-all-start) | async-done | bytes 7340064 | tf_op jit(solution)/shard_map/all_to_all | solution.py:65
  391.8 3.8 convert_add_fusion
  397.5 7.1 %fusion.44 = f32[64,64]{1,0:T(8,128)S(1)} fusion(f32[8192,64]{1,0:T(8,128)S(1)} %convert_add_fusion), kind=kOutput, calls=%fused_computation.88 | convolution fusion | flops 402653184 | bytes 2113536 | tf_op jit(solution)/shard_map/dot_general | solution.py:16
  404.7 5.8 %cholesky.74 = f32[64,64]{1,0:T(8,128)S(1)} custom-call(f32[64,64]{1,0:T(8,128)S(1)} %fusion.36), custom_call_target="Cholesky" | custom-call | tf_op jit(solution)/shard_map/jit(cholesky)/cholesky | solution.py:34
  411.9 4.9 custom-call.10
  417.1 4.4 slice.35
  421.9 5.8 %cholesky.85 = f32[64,64]{1,0:T(8,128)S(1)} custom-call(f32[64,64]{1,0:T(8,128)S(1)} %fusion.34), custom_call_target="Cholesky" | custom-call | tf_op jit(solution)/shard_map/jit(cholesky)/cholesky | solution.py:38
  429.1 4.9 custom-call.11
  434.7 8.3 %fusion.43 = (bf16[8192,64]{0,1:T(8,128)(2,1)S(1)}, f32[8192,64]{0,1:T(8,128)}) fusion(f32[8192,64]{1,0:T(8,128)} %copy-done.1, f32[64,64]{1,0:T(8,128)S(1)} %fusion.47), kind=kOutput, calls=%fused_computation.87 | convolution fusion | flops 403177472 | bytes 5259264 | tf_op jit(solution)/shard_map/dot_general | solution.py:16
  444.1 6.3 %fusion.9 = f32[512,320]{0,1:T(8,128)S(1)} fusion(bf16[128,8192]{1,0:T(8,128)(2,1)} %collective-permute-done.2, bf16[128,8192]{1,0:T(8,128)(2,1)} %collective-permute-done.1, bf16[128,8192]{1,0:T(8,128)(2,1)} %collective-permute-done, bf16[128,8192]{1,0:T(8,128)(2,1)} %bitcast.118, bf16[8192,64]{1,0:T(8,128)(2,1)S(1)} %copy.61, bf16[8192,256]{1,0:T(8,128)(2,1)} %slice.35), kind=kOutput, calls=%fused_computation.15 | convolution fusion | flops 2728394752 | bytes 14286848 | tf_op jit(solution)/shard_map/dot_general | solution.py:87
  452.4 25.5 %while.23 = (s32[]{:T(128)}, f32[2,2]{1,0:T(2,128)S(1)}, bf16[2,8,512,128]{2,3,1,0:T(8,128)(2,1)}, bf16[2,2,512,128]{3,2,1,0:T(8,128)(2,1)S(1)}, s32[512]{0:T(51...) while((s32[]{:T(128)}, f32[2,2]{1,0:T(2,128)S(1)}, ...), condition=%wide.region_9.13_spmd.clone, body=%wide.region_2.12_spmd.clone.sunk | while | flops 138674192 | bytes 10115450 | solution.py:119
  454.7 10.4 %while.24 = (s32[]{:T(128)}, f32[8,2]{1,0:T(8,128)S(1)}, pred[512,512]{0,1:T(8,128)(4,1)S(1)}, bf16[8,512,128]{2,1,0:T(8,128)(2,1)S(1)}, bf16[2,512,128]{2,1,0:T(8,128)(2,1)S(1)}, /*index=5*/s32[]{:T(128)}, s32[]{:T(128)}) while((s32[]{:T(128)}, f32[8,2]{1,0:T(8,128)S(1)}, pred[512,512]{0,1:T(8,128)(4,1)S(1)}, ...), condition=%wide.region_7.10_spmd, body=%wide.region_3.0_spmd.sunk | while | flops 138412032 | bytes 5132397 | solution.py:116
  467.4 10.4 %while.24 = (s32[]{:T(128)}, f32[8,2]{1,0:T(8,128)S(1)}, pred[512,512]{0,1:T(8,128)(4,1)S(1)}, bf16[8,512,128]{2,1,0:T(8,128)(2,1)S(1)}, bf16[2,512,128]{2,1,0:T(8,128)(2,1)S(1)}, /*index=5*/s32[]{:T(128)}, s32[]{:T(128)}) while((s32[]{:T(128)}, f32[8,2]{1,0:T(8,128)S(1)}, pred[512,512]{0,1:T(8,128)(4,1)S(1)}, ...), condition=%wide.region_7.10_spmd, body=%wide.region_3.0_spmd.sunk | while | flops 138412032 | bytes 5132397 | solution.py:116
  478.5 12.2 %all-to-all-start.1 = ((f32[128,1,2]{2,1,0:T(1,128)}), f32[128,1,2]{2,1,0:T(1,128)S(1)}, u32[]{:S(2)}, u32[]{:S(2)}) async-start(f32[128,1,2]{2,1,0:T(1,128)} %broadcast_in_dim.47), calls=%async_computation.1 | async-start | bytes 131072 | tf_op jit(solution)/shard_map/all_to_all | solution.py:54
  492.7 12.9 %all-to-all-done.1 = f32[128,1,2]{2,1,0:T(1,128)S(1)} async-done(((f32[128,1,2]{2,1,0:T(1,128)}), f32[128,1,2]{2,1,0:T(1,128)S(1)}, u32[]{:S(2)}, u32[]{:S(2)}) %all-to-all-start.1) | async-done | bytes 1056 | tf_op jit(solution)/shard_map/all_to_all | solution.py:54
  505.8 7.9 %all_to_all.17 = f32[4,1,2]{2,1,0:T(1,128)S(1)} all-to-all(f32[4,1,2]{2,1,0:T(1,128)S(1)} %broadcast_in_dim.48), channel_id=1, replica_groups=mesh['fsdp'=128,'seq'=4] {'seq'}, dimensions={0} | all-to-all | bytes 64 | tf_op jit(solution)/shard_map/all_to_all | solution.py:54
  (137 shorter events, 49.8 us)
Async XLA Ops:
  0.6 37.7 %copy-start = (f32[1024,64]{0,1:T(8,128)S(1)}, f32[1024,64]{0,1:T(8,128)}, u32[]{:S(2)}) copy-start(f32[1024,64]{0,1:T(8,128)} %param.18) | copy-start | bytes 786436
  6.6 385.2 %all-to-all-start = ((bf16[128,64,448]{2,1,0:T(8,128)(2,1)}), bf16[128,64,448]{2,1,0:T(8,128)(2,1)}, u32[]{:S(2)}, u32[]{:S(2)}) async-start(bf16[128,64,448]{2,1,0:T(8,128)(2,1)} %stack.8), calls=%async_computation | async-start | bytes 16777216 | tf_op jit(solution)/shard_map/all_to_all | solution.py:65
  27.6 36.3 %copy-start.2 = (bf16[1,512,2048]{2,1,0:T(8,128)(2,1)S(1)}, bf16[1,512,2048]{2,1,0:T(8,128)(2,1)}, u32[]{:S(2)}) copy-start(bf16[1,512,2048]{2,1,0:T(8,128)(2,1)} %param.15) | copy-start | bytes 6291460
  27.6 416.5 %collective-permute-start = (bf16[128,8192]{1,0:T(8,128)(2,1)}, bf16[128,8192]{1,0:T(8,128)(2,1)}, u32[]{:S(2)}, u32[]{:S(2)}) collective-permute-start(bf16[128,8192]{1,0:T(8,128)(2,1)} %bitcast.115), channel_id=1, source_target_pairs={{0,1},{1,2},{2,3},{3,0},{4,5},{5,6},{6,7},{7,4},{8,9},{9,10},{10,1... | collective-permute-start | bytes 6291464 | tf_op jit(solution)/shard_map/ppermute | solution.py:72
  30.9 413.3 %collective-permute-start.1 = (bf16[128,8192]{1,0:T(8,128)(2,1)}, bf16[128,8192]{1,0:T(8,128)(2,1)}, u32[]{:S(2)}, u32[]{:S(2)}) collective-permute-start(bf16[128,8192]{1,0:T(8,128)(2,1)} %bitcast.116), channel_id=1, source_target_pairs={{0,2},{1,3},{2,0},{3,1},{4,6},{5,7},{6,4},{7,5},{8,10},{9,11},{10,... | collective-permute-start | bytes 6291464 | tf_op jit(solution)/shard_map/ppermute | solution.py:72
  35.2 408.9 %collective-permute-start.2 = (bf16[128,8192]{1,0:T(8,128)(2,1)}, bf16[128,8192]{1,0:T(8,128)(2,1)}, u32[]{:S(2)}, u32[]{:S(2)}) collective-permute-start(bf16[128,8192]{1,0:T(8,128)(2,1)} %bitcast.117), channel_id=1, source_target_pairs={{0,3},{1,0},{2,1},{3,2},{4,7},{5,4},{6,5},{7,6},{8,11},{9,8},{10,9... | collective-permute-start | bytes 6291464 | tf_op jit(solution)/shard_map/ppermute | solution.py:72
  395.6 2.0 copy-start.1
  452.4 38.4 %copy-start.3 = (f32[1024,64]{0,1:T(8,128)S(1)}, f32[1024,64]{0,1:T(8,128)}, u32[]{:S(2)}) copy-start(f32[1024,64]{0,1:T(8,128)} %convolution_bitcast_fusion) | copy-start | bytes 786436
  478.5 27.1 %all-to-all-start.1 = ((f32[128,1,2]{2,1,0:T(1,128)}), f32[128,1,2]{2,1,0:T(1,128)S(1)}, u32[]{:S(2)}, u32[]{:S(2)}) async-start(f32[128,1,2]{2,1,0:T(1,128)} %broadcast_in_dim.47), calls=%async_computation.1 | async-start | bytes 131072 | tf_op jit(solution)/shard_map/all_to_all | solution.py:54
